TPU v7x, 256 devices: a whole 4x4x8 slice. The times are simulated.
256 devices in a mesh: hid: 32 (over z_hi, x, core), wid: 8 (over z_lo, y).
Axes of the slice: x: 4, y: 4, z: 8 (z_hi: 4, z_lo: 2; z = z_hi * 2 + z_lo), core: 2. Of those that a mesh axis runs over, the one named last changes fastest.
Arguments:
- inputs: bfloat16 [768, 8192], P('hid', 'wid'), may hold values from -6 to 6
- gate_weight: bfloat16 [8192, 28672], P('wid', 'hid'), may hold values from -0.0625 to 0.0625
- up_weight: bfloat16 [8192, 28672], P('wid', 'hid'), may hold values from -0.0625 to 0.0625
- down_weight: bfloat16 [28672, 8192], P('hid', 'wid'), may hold values from -0.03125 to 0.03125
- out_grad: bfloat16 [768, 8192], P('hid', 'wid'), may hold values from -0.43164062 to 0.43164062
Outputs:
- input_grad: bfloat16 [768, 8192], P('hid', 'wid')
- gate_grad: bfloat16 [8192, 28672], P('wid', 'hid')
- up_grad: bfloat16 [8192, 28672], P('wid', 'hid')
- down_grad: bfloat16 [28672, 8192], P('hid', 'wid')
All inputs are finite; a program needn't handle non-finite values.
Results may differ from a plain program's by a relative error of at most 0.02.
Values may be sent and summed in bfloat16 or wider, within the bound.
No kernel may reach another device: no remote copies, remote signals or barrier semaphores. Data moves between devices by JAX's collectives and lax.ppermute only.
A program may use at most 64 MiB of HBM per device.

v0:
```python
import jax
import jax.numpy as jnp
from jax import lax
from jax.sharding import Mesh, PartitionSpec as P


def swiglu_terms(gate, up, hidden_grad):
    sigma = jax.nn.sigmoid(gate)
    hidden = (gate * sigma * up).astype(jnp.bfloat16)
    up_term = (hidden_grad * gate * sigma).astype(jnp.bfloat16)
    gate_term = (hidden_grad * up * sigma * (1.0 + gate * (1.0 - sigma))).astype(jnp.bfloat16)
    return (hidden, gate_term, up_term)


def make_per_device(n_hid, n_wid):

    def per_device(inputs, gate_weight, up_weight, down_weight, out_grad):
        dw = inputs.shape[1]
        ff = gate_weight.shape[1]
        both = lax.all_gather(
            jnp.concatenate([inputs, out_grad], 1), ("chip", "core"), axis=0, tiled=True
        )
        all_inputs, all_grads = (both[:, :dw], both[:, dw:])
        tokens = all_inputs.shape[0]
        contract_last = (((1,), (1,)), ((), ()))
        gate_part = jnp.dot(all_inputs, gate_weight, preferred_element_type=jnp.float32)
        up_part = jnp.dot(all_inputs, up_weight, preferred_element_type=jnp.float32)
        grad_part = lax.dot_general(
            all_grads, down_weight, contract_last, preferred_element_type=jnp.float32
        )
        parts = jnp.concatenate([gate_part, up_part, grad_part], 1).astype(jnp.bfloat16)
        parts = lax.all_to_all(
            parts.reshape(n_wid, tokens // n_wid, 3 * ff), "wid", 0, 0, tiled=False
        )
        sums = jnp.sum(parts.astype(jnp.float32), 0)
        gate, up, hidden_grad = (sums[:, :ff], sums[:, ff : 2 * ff], sums[:, 2 * ff :])
        hidden, gate_term, up_term = swiglu_terms(gate, up, hidden_grad)
        hidden = lax.all_gather(hidden, "wid", axis=0, tiled=True)
        terms = jnp.concatenate([gate_term, up_term], 1)
        terms = jnp.broadcast_to(terms[None], (n_wid,) + terms.shape)
        terms = lax.all_to_all(terms, "wid", 0, 0, tiled=False).reshape(tokens, 2 * ff)
        gate_term, up_term = (terms[:, :ff], terms[:, ff:])
        core = lax.axis_index("core")
        by_core = (n_hid // 2, 2, tokens // n_hid, ff)

        def rows_of(which):
            g = lax.dynamic_index_in_dim(gate_term.reshape(by_core), which, 1, keepdims=False)
            u = lax.dynamic_index_in_dim(up_term.reshape(by_core), which, 1, keepdims=False)
            return lax.dot_general(
                g.reshape(-1, ff), gate_weight, contract_last, preferred_element_type=jnp.float32
            ) + lax.dot_general(
                u.reshape(-1, ff), up_weight, contract_last, preferred_element_type=jnp.float32
            )

        sent = lax.ppermute(rows_of(1 - core).astype(jnp.bfloat16), "core", [(0, 1), (1, 0)])
        total = rows_of(core) + sent.astype(jnp.float32)
        total = total.reshape(n_hid // 2, tokens // n_hid, dw)
        total = lax.all_to_all(total.astype(jnp.bfloat16), "chip", 0, 0, tiled=False)
        input_grad = jnp.sum(total.astype(jnp.float32), 0).astype(jnp.bfloat16)
        contract_first = (((0,), (0,)), ((), ()))
        gate_grad = lax.dot_general(
            all_inputs, gate_term, contract_first, preferred_element_type=jnp.float32
        ).astype(jnp.bfloat16)
        up_grad = lax.dot_general(
            all_inputs, up_term, contract_first, preferred_element_type=jnp.float32
        ).astype(jnp.bfloat16)
        down_grad = lax.dot_general(
            hidden, all_grads, contract_first, preferred_element_type=jnp.float32
        ).astype(jnp.bfloat16)
        return (input_grad, gate_grad, up_grad, down_grad)

    return per_device


def solution(mesh):
    n_hid, n_wid = (mesh.shape["hid"], mesh.shape["wid"])
    split = Mesh(mesh.devices.reshape(n_hid // 2, 2, n_wid), ("chip", "core", "wid"))
    hid = ("chip", "core")
    placed = (P(hid, "wid"), P("wid", hid), P("wid", hid), P(hid, "wid"), P(hid, "wid"))
    return jax.shard_map(
        make_per_device(n_hid, n_wid),
        mesh=split,
        in_specs=placed,
        out_specs=(P(hid, "wid"), P("wid", hid), P("wid", hid), P(hid, "wid")),
        check_vma=False,
    )
```

profile of v0, /device:TPU:32, one launch (start us, length us, event | category | flops | bytes accessed | tf_op | source)
XLA Modules:
  0.0 225.8 jit_solution(1284275522411784669)
XLA Ops:
  7.2 0.0 copy-start
  7.2 0.0 all-gather.3.cloned.1.call-start
  7.2 1.6 pad_maximum_fusion.2
  8.8 0.0 all-gather.3.cloned.1.call-update
  8.8 60.5 %all-gather.3.cloned.1.call-done = bf16[768,2048]{1,0:T(8,128)(2,1)} async-done(((bf16[24,2048]{1,0:T(8,128)(2,1)}), bf16[768,2048]{1,0:T(8,128)(2,1)}) %all-gather.3.cloned.1.call-update) | async-done | bytes 3145744 | tf_op jit(solution)/shard_map/all_gather | solution.py:20
  69.3 0.0 copy-start.1
  69.3 0.0 copy-start.3
  69.4 3.9 %convolution_convert_fusion.4 = bf16[768,896]{1,0:T(8,128)(2,1)S(1)} fusion(bf16[1024,896]{1,0:T(8,128)(2,1)} %param.7, bf16[768,2048]{1,0:T(8,128)(2,1)} %all-gather.3.cloned.1.call-done), kind=kOutput, calls=%fused_computation.6 | convolution fusion | flops 1409974272 | bytes 4784128 | tf_op jit(solution)/shard_map/dot_general | solution.py:27
  73.3 0.0 copy-done.1
  73.3 0.0 copy-done.3
  73.3 1.9 convolution_convert_fusion.3
  75.2 0.0 copy-done
  75.2 1.8 convolution_convert_fusion.5
  77.0 0.4 pad_maximum_fusion
  77.3 54.2 %all_to_all.15 = bf16[8,96,2688]{2,1,0:T(8,128)(2,1)S(1)} all-to-all(bf16[8,96,2688]{2,1,0:T(8,128)(2,1)S(1)} %pad_maximum_fusion), channel_id=1, replica_groups=mesh['chip'=16,'core'=2,'wid'=8] {'wid'}, dimensions={0} | all-to-all | bytes 8257536 | tf_op jit(solution)/shard_map/all_to_all | solution.py:32
  131.5 0.5 convert_reduce_fusion
  132.1 0.9 multiply_convert_fusion
  133.0 1.8 broadcast_in_dim.2
  134.7 5.7 %all-to-all-start.1 = ((bf16[8,96,1792]{2,1,0:T(8,128)(2,1)}), bf16[8,96,1792]{2,1,0:T(8,128)(2,1)}, u32[]{:S(2)}, u32[]{:S(2)}) async-start(bf16[8,96,1792]{2,1,0:T(8,128)(2,1)} %broadcast_in_dim.2), calls=%async_computation.1 | async-start | bytes 5505024 | tf_op jit(solution)/shard_map/all_to_all | solution.py:41
  140.5 0.0 all-gather.5.cloned.1.call-start
  140.5 0.7 all-gather.5.cloned.1.call-update
  141.2 37.8 %all-to-all-done.1 = bf16[8,96,1792]{2,1,0:T(8,128)(2,1)} async-done(((bf16[8,96,1792]{2,1,0:T(8,128)(2,1)}), bf16[8,96,1792]{2,1,0:T(8,128)(2,1)}, u32[]{:S(2)}, u32[]{:S(2)}) %all-to-all-start.1) | async-done | bytes 2752544 | tf_op jit(solution)/shard_map/all_to_all | solution.py:41
  179.0 2.0 fusion.8
  181.0 0.3 constant_dynamic-slice_fusion.2
  181.3 0.0 copy-start.4
  181.3 1.0 fusion.10
  182.3 0.5 copy-done.4
  182.8 1.0 add_convert_fusion.1
  183.8 0.1 collective-permute-start
  183.9 1.0 fusion.9
  184.9 1.2 collective-permute-done
  186.2 1.9 add_convert_fusion
  188.1 5.6 %all-to-all-start.2 = ((bf16[16,24,1024]{2,1,0:T(8,128)(2,1)}), bf16[16,24,1024]{2,1,0:T(8,128)(2,1)S(1)}, u32[]{:S(2)}, u32[]{:S(2)}) async-start(bf16[16,24,1024]{2,1,0:T(8,128)(2,1)} %bitcast.10), calls=%async_computation.2 | async-start | bytes 1572864 | tf_op jit(solution)/shard_map/all_to_all | solution.py:58
  193.6 0.0 all-gather.5.cloned.1.call-done
  193.7 0.0 copy-start.2
  193.7 4.8 %convolution_convert_fusion = bf16[896,1024]{1,0:T(8,128)(2,1)} fusion(bf16[768,896]{1,0:T(8,128)(2,1)} %all-gather.5.cloned.1.call-done, bf16[768,2048]{1,0:T(8,128)(2,1)} %all-gather.3.cloned.1.call-done), kind=kOutput, calls=%fused_computation.2 | convolution fusion | flops 1410203648 | bytes 4784128 | tf_op jit(solution)/shard_map/dot_general | solution.py:67
  198.5 0.0 copy-done.2
  198.5 4.4 %convolution_convert_fusion.1 = bf16[1024,896]{1,0:T(8,128)(2,1)} fusion(bf16[768,2048]{1,0:T(8,128)(2,1)S(1)} %copy-done.2, bf16[768,1792]{1,0:T(8,128)(2,1)} %bitcast.3), kind=kOutput, calls=%fused_computation.3 | convolution fusion | flops 1410203648 | bytes 4784128 | tf_op jit(solution)/shard_map/dot_general | solution.py:64
  202.9 4.4 %convolution_convert_fusion.2 = bf16[1024,896]{1,0:T(8,128)(2,1)} fusion(bf16[768,2048]{1,0:T(8,128)(2,1)S(1)} %copy-done.2, bf16[768,1792]{1,0:T(8,128)(2,1)} %bitcast.3), kind=kOutput, calls=%fused_computation.4 | convolution fusion | flops 1410203648 | bytes 4784128 | tf_op jit(solution)/shard_map/dot_general | solution.py:61
  207.4 10.9 %all-to-all-done.2 = bf16[16,24,1024]{2,1,0:T(8,128)(2,1)S(1)} async-done(((bf16[16,24,1024]{2,1,0:T(8,128)(2,1)}), bf16[16,24,1024]{2,1,0:T(8,128)(2,1)S(1)}, u32[]{:S(2)}, u32[]{:S(2)}) %all-to-all-start.2) | async-done | bytes 786464 | tf_op jit(solution)/shard_map/all_to_all | solution.py:58
  218.2 0.7 reduce_sum.22
  (1 shorter events, 0.0 us)
Async XLA Ops:
  7.2 68.0 %copy-start = (bf16[1024,896]{1,0:T(8,128)(2,1)S(1)}, bf16[1024,896]{1,0:T(8,128)(2,1)}, u32[]{:S(2)}) copy-start(bf16[1024,896]{1,0:T(8,128)(2,1)} %param.6) | copy-start | bytes 5505028
  7.2 62.2 %all-gather.3.cloned.1.call-start = ((), (), s32[]{:S(2)}) async-start(), calls=%async_computation.3 | async-start | bytes 3244032 | tf_op jit(solution)/shard_map/all_gather | solution.py:20
  69.3 3.9 %copy-start.1 = (bf16[768,2048]{1,0:T(8,128)(2,1)S(1)}, bf16[768,2048]{1,0:T(8,128)(2,1)}, u32[]{:S(2)}) copy-start(bf16[768,2048]{1,0:T(8,128)(2,1)} %all-gather.3.cloned.1.call-done) | copy-start | bytes 9437188
  69.3 3.9 %copy-start.3 = (bf16[896,1024]{1,0:T(8,128)(2,1)S(1)}, bf16[896,1024]{1,0:T(8,128)(2,1)}, u32[]{:S(2)}) copy-start(bf16[896,1024]{1,0:T(8,128)(2,1)} %param.8) | copy-start | bytes 5505028
  134.7 44.3 %all-to-all-start.1 = ((bf16[8,96,1792]{2,1,0:T(8,128)(2,1)}), bf16[8,96,1792]{2,1,0:T(8,128)(2,1)}, u32[]{:S(2)}, u32[]{:S(2)}) async-start(bf16[8,96,1792]{2,1,0:T(8,128)(2,1)} %broadcast_in_dim.2), calls=%async_computation.1 | async-start | bytes 5505024 | tf_op jit(solution)/shard_map/all_to_all | solution.py:41
  140.5 53.2 %all-gather.5.cloned.1.call-start = ((), (), s32[]{:S(2)}) async-start(), calls=%async_computation.4 | async-start | bytes 1548288 | tf_op jit(solution)/shard_map/all_gather | solution.py:38
  181.3 1.5 copy-start.4
  183.8 2.4 %collective-permute-start = (bf16[384,1024]{1,0:T(8,128)(2,1)S(1)}, bf16[384,1024]{1,0:T(8,128)(2,1)S(1)}, u32[]{:S(2)}, u32[]{:S(2)}) collective-permute-start(bf16[384,1024]{1,0:T(8,128)(2,1)S(1)} %add_convert_fusion.1), channel_id=1, source_target_pairs={{0,8},{8,0},{1,9},{9,1},{2,10},{10,2},{3,11},{11,3},{4,12},{12,4},... | collective-permute-start | bytes 2359304 | tf_op jit(solution)/shard_map/ppermute | solution.py:55
  188.1 30.2 %all-to-all-start.2 = ((bf16[16,24,1024]{2,1,0:T(8,128)(2,1)}), bf16[16,24,1024]{2,1,0:T(8,128)(2,1)S(1)}, u32[]{:S(2)}, u32[]{:S(2)}) async-start(bf16[16,24,1024]{2,1,0:T(8,128)(2,1)} %bitcast.10), calls=%async_computation.2 | async-start | bytes 1572864 | tf_op jit(solution)/shard_map/all_to_all | solution.py:58
  193.7 4.8 %copy-start.2 = (bf16[768,2048]{1,0:T(8,128)(2,1)S(1)}, bf16[768,2048]{1,0:T(8,128)(2,1)}, u32[]{:S(2)}) copy-start(bf16[768,2048]{1,0:T(8,128)(2,1)} %all-gather.3.cloned.1.call-done) | copy-start | bytes 9437188
Sparse Core Ops, SparseCore 0:
  11.1 58.1 all-gather.2
  143.7 48.2 all-gather.4
where the time goes:
time: 226 us
  waiting for transfers between devices  111 us (49%)
  blocking collectives  54.2 us (24%)
  matrix products  26.2 us (12%)
  between operations  14.2 us (6%)
  starting transfers between devices  11.4 us (5%)
  local copies, waits for them, and re-layouts  4.54 us (2%)
  other arithmetic  4.13 us (2%)
    all_gather x1, waiting for transfers between devices, per_device(): lax.all_gather(jnp.concatenate([inputs, out_grad], 1), ('chip', 'core'),...  60.5 us
    all_to_all x1, blocking collectives, per_device(): lax.all_to_all(parts.reshape(n_wid, tokens // n_wid, 3 * ff), 'wid', 0, 0...  54.2 us
    all_to_all x1, waiting for transfers between devices, per_device(): lax.all_to_all(terms, 'wid', 0, 0, tiled=False).reshape(tokens, 2 * ff)  37.8 us
    all_to_all x1, waiting for transfers between devices, per_device(): lax.all_to_all(total.astype(jnp.bfloat16), 'chip', 0, 0, tiled=False)  10.9 us
    all_to_all x1, starting transfers between devices, per_device(): lax.all_to_all(terms, 'wid', 0, 0, tiled=False).reshape(tokens, 2 * ff)  5.75 us
    all_to_all x1, starting transfers between devices, per_device(): lax.all_to_all(total.astype(jnp.bfloat16), 'chip', 0, 0, tiled=False)  5.56 us
    dot_general x1, matrix products, per_device(): lax.dot_general(hidden, all_grads, contract_first, preferred_element_type...  4.83 us
  transfers between devices with their start and end apart: 5, of which 4 were waited for; matrix products, arithmetic and copies ran while one was open for 9% of the time, Pallas kernels for 0%

commit v1 on v0

--- a/solution.py
+++ b/solution.py
@@ -17,9 +17,14 @@
     def per_device(inputs, gate_weight, up_weight, down_weight, out_grad):
         dw = inputs.shape[1]
         ff = gate_weight.shape[1]
-        both = lax.all_gather(
-            jnp.concatenate([inputs, out_grad], 1), ("chip", "core"), axis=0, tiled=True
+        my_tile = jnp.concatenate([inputs, out_grad], 1)
+        block_out = lax.all_to_all(
+            jnp.stack([my_tile for _ in range(lax.axis_size(("chip", "core")))]),
+            ("chip", "core"),
+            0,
+            0,
         )
+        both = jnp.concatenate(block_out, axis=0)
         all_inputs, all_grads = (both[:, :dw], both[:, dw:])
         tokens = all_inputs.shape[0]
         contract_last = (((1,), (1,)), ((), ()))

time: 226 us -> 247 us (1.093)
  blocking collectives: 54.2 us -> 138 us
  waiting for transfers between devices: 111 us -> 50.6 us
    all_to_all x0 -> x1, blocking collectives: none -> 84.2 us  [per_device(): lax.all_to_all(jnp.stack([my_tile for _ in range(lax.axis_size(('chip', '...]
    all_gather x1 -> x0, waiting for transfers between devices: 60.5 us -> none  [per_device(): lax.all_gather(jnp.concatenate([inputs, out_grad], 1), ('chip', 'core'),...]
  transfers between devices with their start and end apart: 5 -> 4, of which waited for: 4 -> 3; matrix products, arithmetic and copies ran while one was open for 9% -> 8% of each run, Pallas kernels for 0% -> 0%
where the time goes in v1:
time: 247 us; the launch traced here: 246 us
  blocking collectives  138 us (56%)
  waiting for transfers between devices  50.6 us (20%)
  matrix products  24.1 us (10%)
  between operations  14.2 us (6%)
  starting transfers between devices  10.2 us (4%)
  local copies, waits for them, and re-layouts  5.73 us (2%)
  other arithmetic  3.5 us (1%)
    all_to_all x1, blocking collectives, per_device(): lax.all_to_all(jnp.stack([my_tile for _ in range(lax.axis_size(('chip', '...  84.2 us
    all_to_all x1, blocking collectives, per_device(): lax.all_to_all(parts.reshape(n_wid, tokens // n_wid, 3 * ff), 'wid', 0, 0...  53.6 us
    all_to_all x1, waiting for transfers between devices, per_device(): lax.all_to_all(terms, 'wid', 0, 0, tiled=False).reshape(tokens, 2 * ff)  37.8 us
    all_to_all x1, waiting for transfers between devices, per_device(): lax.all_to_all(total.astype(jnp.bfloat16), 'chip', 0, 0, tiled=False)  10.8 us
    all_to_all x1, starting transfers between devices, per_device(): lax.all_to_all(terms, 'wid', 0, 0, tiled=False).reshape(tokens, 2 * ff)  5.74 us
  transfers between devices with their start and end apart: 4, of which 3 were waited for; matrix products, arithmetic and copies ran while one was open for 8% of the time, Pallas kernels for 0%

profile of v1, /device:TPU:32, one launch (start us, length us, event | category | flops | bytes accessed | tf_op | source)
XLA Modules:
  0.0 246.1 jit_solution(5362807264249497648)
XLA Ops:
  7.2 0.0 copy-start
  7.2 1.0 pad_maximum_fusion.2
  8.1 0.4 stack.2
  8.5 0.0 copy-start.4
  8.5 84.2 %all_to_all.20 = bf16[32,24,2048]{2,1,0:T(8,128)(2,1)S(1)} all-to-all(bf16[32,24,2048]{2,1,0:T(8,128)(2,1)S(1)} %stack.2), channel_id=1, replica_groups=mesh['chip'=16,'core'=2,'wid'=8] {'chip','core'}, dimensions={0} | all-to-all | bytes 6291456 | tf_op jit(solution)/shard_map/all_to_all | solution.py:21
  92.8 0.0 copy-start.1
  92.8 0.0 copy-done.4
  92.8 0.0 copy-start.3
  92.8 1.8 convolution_convert_fusion.4
  94.6 0.8 copy-done.3
  95.4 1.9 convolution_convert_fusion.3
  97.3 0.0 copy-done.1
  97.3 0.0 copy-done
  97.3 1.8 convolution_convert_fusion.5
  99.1 0.4 pad_maximum_fusion
  99.5 53.6 %all_to_all.21 = bf16[8,96,2688]{2,1,0:T(8,128)(2,1)S(1)} all-to-all(bf16[8,96,2688]{2,1,0:T(8,128)(2,1)S(1)} %pad_maximum_fusion), channel_id=1, replica_groups=mesh['chip'=16,'core'=2,'wid'=8] {'wid'}, dimensions={0} | all-to-all | bytes 8257536 | tf_op jit(solution)/shard_map/all_to_all | solution.py:37
  153.0 0.5 convert_reduce_fusion
  153.6 0.9 multiply_convert_fusion
  154.5 1.8 broadcast_in_dim.2
  156.2 5.7 %all-to-all-start.2 = ((bf16[8,96,1792]{2,1,0:T(8,128)(2,1)}), bf16[8,96,1792]{2,1,0:T(8,128)(2,1)}, u32[]{:S(2)}, u32[]{:S(2)}) async-start(bf16[8,96,1792]{2,1,0:T(8,128)(2,1)} %broadcast_in_dim.2), calls=%async_computation.2 | async-start | bytes 5505024 | tf_op jit(solution)/shard_map/all_to_all | solution.py:46
  162.0 0.0 all-gather.2.cloned.1.call-start
  162.0 0.7 all-gather.2.cloned.1.call-update
  162.7 37.8 %all-to-all-done.2 = bf16[8,96,1792]{2,1,0:T(8,128)(2,1)} async-done(((bf16[8,96,1792]{2,1,0:T(8,128)(2,1)}), bf16[8,96,1792]{2,1,0:T(8,128)(2,1)}, u32[]{:S(2)}, u32[]{:S(2)}) %all-to-all-start.2) | async-done | bytes 2752544 | tf_op jit(solution)/shard_map/all_to_all | solution.py:46
  200.5 2.0 fusion.8
  202.5 0.3 constant_dynamic-slice_fusion.2
  202.8 0.0 copy-start.5
  202.8 1.0 fusion.10
  203.8 0.5 copy-done.5
  204.3 1.0 add_convert_fusion.1
  205.3 0.1 collective-permute-start
  205.4 1.0 fusion.9
  206.4 1.2 collective-permute-done
  207.7 1.9 add_convert_fusion
  209.6 4.4 %all-to-all-start.3 = ((bf16[16,24,1024]{2,1,0:T(8,128)(2,1)}), bf16[16,24,1024]{2,1,0:T(8,128)(2,1)S(1)}, u32[]{:S(2)}, u32[]{:S(2)}) async-start(bf16[16,24,1024]{2,1,0:T(8,128)(2,1)} %bitcast.11), calls=%async_computation.3 | async-start | bytes 1572864 | tf_op jit(solution)/shard_map/all_to_all | solution.py:63
  214.0 0.0 all-gather.2.cloned.1.call-done
  214.0 0.0 copy-start.2
  214.0 4.8 %convolution_convert_fusion = bf16[896,1024]{1,0:T(8,128)(2,1)} fusion(bf16[768,896]{1,0:T(8,128)(2,1)} %all-gather.2.cloned.1.call-done, bf16[768,2048]{1,0:T(8,128)(2,1)} %bitcast.29), kind=kOutput, calls=%fused_computation.2 | convolution fusion | flops 1410203648 | bytes 4784128 | tf_op jit(solution)/shard_map/dot_general | solution.py:72
  218.8 0.0 copy-done.2
  218.8 4.4 %convolution_convert_fusion.1 = bf16[1024,896]{1,0:T(8,128)(2,1)} fusion(bf16[768,2048]{1,0:T(8,128)(2,1)S(1)} %bitcast.30, bf16[768,1792]{1,0:T(8,128)(2,1)} %bitcast.4), kind=kOutput, calls=%fused_computation.3 | convolution fusion | flops 1410203648 | bytes 4784128 | tf_op jit(solution)/shard_map/dot_general | solution.py:69
  223.3 4.4 %convolution_convert_fusion.2 = bf16[1024,896]{1,0:T(8,128)(2,1)} fusion(bf16[768,2048]{1,0:T(8,128)(2,1)S(1)} %bitcast.31, bf16[768,1792]{1,0:T(8,128)(2,1)} %bitcast.4), kind=kOutput, calls=%fused_computation.4 | convolution fusion | flops 1410203648 | bytes 4784128 | tf_op jit(solution)/shard_map/dot_general | solution.py:66
  227.7 10.8 %all-to-all-done.3 = bf16[16,24,1024]{2,1,0:T(8,128)(2,1)S(1)} async-done(((bf16[16,24,1024]{2,1,0:T(8,128)(2,1)}), bf16[16,24,1024]{2,1,0:T(8,128)(2,1)S(1)}, u32[]{:S(2)}, u32[]{:S(2)}) %all-to-all-start.3) | async-done | bytes 786464 | tf_op jit(solution)/shard_map/all_to_all | solution.py:63
  238.5 0.7 reduce_sum.22
  (1 shorter events, 0.0 us)
Async XLA Ops:
  7.2 90.1 %copy-start = (bf16[1024,896]{1,0:T(8,128)(2,1)S(1)}, bf16[1024,896]{1,0:T(8,128)(2,1)}, u32[]{:S(2)}) copy-start(bf16[1024,896]{1,0:T(8,128)(2,1)} %param.6) | copy-start | bytes 5505028
  8.5 84.2 %copy-start.4 = (bf16[1024,896]{1,0:T(8,128)(2,1)S(1)}, bf16[1024,896]{1,0:T(8,128)(2,1)}, u32[]{:S(2)}) copy-start(bf16[1024,896]{1,0:T(8,128)(2,1)} %param.7) | copy-start | bytes 5505028
  92.8 4.5 %copy-start.1 = (bf16[32,24,2048]{2,1,0:T(8,128)(2,1)}, bf16[32,24,2048]{2,1,0:T(8,128)(2,1)S(1)}, u32[]{:S(2)}) copy-start(bf16[32,24,2048]{2,1,0:T(8,128)(2,1)S(1)} %all_to_all.20) | copy-start | bytes 9437188
  92.8 2.6 %copy-start.3 = (bf16[896,1024]{1,0:T(8,128)(2,1)S(1)}, bf16[896,1024]{1,0:T(8,128)(2,1)}, u32[]{:S(2)}) copy-start(bf16[896,1024]{1,0:T(8,128)(2,1)} %param.8) | copy-start | bytes 5505028
  156.2 44.3 %all-to-all-start.2 = ((bf16[8,96,1792]{2,1,0:T(8,128)(2,1)}), bf16[8,96,1792]{2,1,0:T(8,128)(2,1)}, u32[]{:S(2)}, u32[]{:S(2)}) async-start(bf16[8,96,1792]{2,1,0:T(8,128)(2,1)} %broadcast_in_dim.2), calls=%async_computation.2 | async-start | bytes 5505024 | tf_op jit(solution)/shard_map/all_to_all | solution.py:46
  162.0 52.0 %all-gather.2.cloned.1.call-start = ((), (), s32[]{:S(2)}) async-start(), calls=%async_computation.4 | async-start | bytes 1548288 | tf_op jit(solution)/shard_map/all_gather | solution.py:43
  202.8 1.5 copy-start.5
  205.3 2.4 collective-permute-start
  209.6 28.9 %all-to-all-start.3 = ((bf16[16,24,1024]{2,1,0:T(8,128)(2,1)}), bf16[16,24,1024]{2,1,0:T(8,128)(2,1)S(1)}, u32[]{:S(2)}, u32[]{:S(2)}) async-start(bf16[16,24,1024]{2,1,0:T(8,128)(2,1)} %bitcast.11), calls=%async_computation.3 | async-start | bytes 1572864 | tf_op jit(solution)/shard_map/all_to_all | solution.py:63
  214.0 4.8 %copy-start.2 = (bf16[32,24,2048]{2,1,0:T(8,128)(2,1)S(1)}, bf16[32,24,2048]{2,1,0:T(8,128)(2,1)}, u32[]{:S(2)}) copy-start(bf16[32,24,2048]{2,1,0:T(8,128)(2,1)} %copy-done.1) | copy-start | bytes 9437188
Sparse Core Ops, SparseCore 0:
  165.1 48.2 all-gather.1
